TPU v7x, 512 devices: a whole 4x4x16 slice. The times are simulated.
512 devices in a mesh: dp: 16 (over y_lo, x, core), mp: 32 (over z, y_hi).
Axes of the slice: x: 4, y: 4 (y_hi: 2, y_lo: 2; y = y_hi * 2 + y_lo), z: 16, core: 2. Of those that a mesh axis runs over, the one named last changes fastest.
Arguments:
- hidden_states: bfloat16 [8192, 2560], P(('dp', 'mp')), may hold values from -60 to 60
- norm_gain: float32 [2560], replicated, may hold values from 0.5 to 1.5
- head_weight: bfloat16 [2560, 65536], P(None, ('dp', 'mp')), may hold values from -64 to 64
- target_ids: int32 [8192], P(('dp', 'mp')), may hold values from 0 to 65535
- response_mask: int32 [8192], P(('dp', 'mp')), may hold values from 0 to 1, as said below
Outputs:
- token_logprob: float32 [8192], P(('dp', 'mp'))
- token_entropy: float32 [8192], P(('dp', 'mp'))
Inputs may be any that keep to these rules, and one draw needn't show every extreme that they name: `response_mask`: each aligned run of 256 positions is one rollout: a prompt of 0s, then one span of 1s, then padding 0s.
All inputs are finite; a program needn't handle non-finite values.
Results may differ from a plain program's by a relative error of at most 0.0048.
Values may be sent and summed in bfloat16 or wider, within the bound.
No kernel may reach another device: no remote copies, remote signals or barrier semaphores. Data moves between devices by JAX's collectives and lax.ppermute only.
A program may use at most 64 MiB of HBM per device.

v0:
```python
import jax
import jax.numpy as jnp
from jax import lax
from jax.sharding import Mesh, PartitionSpec as P

id_base = 256
dp_axes = ("ylo", "x", "core")
mp_axes = ("z", "yhi")
every = dp_axes + mp_axes


def shift(value, axis, step):
    count = lax.axis_size(axis)
    return lax.ppermute(value, axis, [(i, (i + step) % count) for i in range(count)])


def block_stats(group, column_piece, column_ids, width):
    group_states = group[:, :width]
    group_targets = (
        group[:, width].astype(jnp.int32) * id_base + group[:, width + 1].astype(jnp.int32)
    )
    logits = jnp.dot(group_states, column_piece, preferred_element_type=jnp.float32)
    top = jnp.max(logits, axis=1)
    shifted = jnp.exp(logits - top[:, None])
    total = jnp.sum(shifted, axis=1)
    moment = jnp.sum(shifted * logits, axis=1)
    hit = group_targets[:, None] == column_ids[None, :]
    chosen = jnp.sum(jnp.where(hit, logits, 0.0), axis=1)
    part_lse = top + jnp.log(total)
    part_expected = moment / total
    return jnp.stack([part_lse, part_expected, chosen], axis=0)


def local(hidden_states, norm_gain, head_weight, target_ids, response_mask):
    states = hidden_states.astype(jnp.float32)
    mean_square = jnp.mean(states * states, axis=1, keepdims=True)
    normed = (states * lax.rsqrt(mean_square + 1e-06) * norm_gain[None, :]).astype(jnp.bfloat16)
    width = normed.shape[1]
    mp_count = lax.axis_size(mp_axes)
    mp_index = lax.axis_index(mp_axes)
    shard_cols = head_weight.shape[1]
    send_count = normed.shape[0]
    id_high = (target_ids // id_base).astype(jnp.bfloat16)
    id_low = (target_ids % id_base).astype(jnp.bfloat16)
    packed = jnp.concatenate([normed, id_high[:, None], id_low[:, None]], axis=1)
    z_count = lax.axis_size("z")
    z_index = lax.axis_index("z")
    yhi_index = lax.axis_index("yhi")
    pair = jnp.concatenate([packed, shift(packed, "yhi", 1)], axis=0)
    ahead = pair
    behind = pair
    blocks = [pair]
    returning = []
    for _ in range(1, z_count // 2):
        ahead = shift(ahead, "z", 1)
        behind = shift(behind, "z", -1)
        blocks.append(ahead)
        returning.append(behind)
    blocks.append(shift(ahead, "z", 1))
    ordered = blocks + returning[::-1]
    chip_piece = lax.all_gather(head_weight, ("ylo", "x"), axis=1, tiled=True)
    other_piece = shift(chip_piece, "core", 1)
    column_piece = jnp.concatenate([chip_piece, other_piece], axis=1)
    core_index = lax.axis_index("core")
    positions = jnp.arange(column_piece.shape[1], dtype=jnp.int32)
    half = positions // chip_piece.shape[1]
    within = positions % chip_piece.shape[1]
    owners = (within // shard_cols) * 2 + (half + core_index) % 2
    column_ids = (owners * mp_count + mp_index) * shard_cols + within % shard_cols
    late = (z_count // 2 - 1, z_count // 2, z_count // 2 + 1)
    early = [k for k in range(z_count) if k not in late]
    early_stats = block_stats(
        jnp.concatenate([ordered[k] for k in early], axis=0), column_piece, column_ids, width
    )
    late_stats = block_stats(
        jnp.concatenate([ordered[k] for k in late], axis=0), column_piece, column_ids, width
    )
    block_rows = pair.shape[0]
    pieces = {}
    for i, k in enumerate(early):
        pieces[k] = early_stats[:, i * block_rows:(i + 1) * block_rows]
    for i, k in enumerate(late):
        pieces[k] = late_stats[:, i * block_rows:(i + 1) * block_rows]
    stats = jnp.concatenate([pieces[k] for k in range(z_count)], axis=1)
    stats = stats.reshape(3, mp_count, send_count)
    owner = jnp.arange(mp_count, dtype=jnp.int32)
    source = ((z_index - owner // 2) % z_count) * 2 + (owner % 2 + yhi_index) % 2
    stats = jnp.take(stats, source, axis=1)
    got = lax.all_to_all(stats, mp_axes, split_axis=1, concat_axis=1, tiled=True)
    lse_parts, expected_parts, chosen_parts = got[0], got[1], got[2]
    top_lse = jnp.max(lse_parts, axis=0)
    log_total = top_lse + jnp.log(jnp.sum(jnp.exp(lse_parts - top_lse[None, :]), axis=0))
    weights = jnp.exp(lse_parts - log_total[None, :])
    expected = jnp.sum(weights * expected_parts, axis=0)
    chosen_logit = jnp.sum(chosen_parts, axis=0)

    scored = response_mask.astype(jnp.float32)
    return ((chosen_logit - log_total) * scored, (log_total - expected) * scored)


def split_mesh(mesh):
    dp_size, mp_size = mesh.devices.shape
    shape = (2, dp_size // 4, 2, mp_size // 2, 2)
    return Mesh(mesh.devices.reshape(shape), every)


def solution(mesh):
    return jax.shard_map(
        local,
        mesh=split_mesh(mesh),
        in_specs=(
            P(every, None),
            P(),
            P(None, every),
            P(every),
            P(every),
        ),
        out_specs=(P(every), P(every)),
        check_vma=False,
    )
```

profile of v0, /device:TPU:6, one launch (start us, length us, event | category | flops | bytes accessed | tf_op | source)
XLA Modules:
  0.0 188.2 jit_solution(5053847019755018815)
XLA Ops:
  7.2 0.7 all-gather.2.cloned.1.call-update
  7.9 0.7 fusion.35
  8.6 0.1 copy.10
  8.7 0.1 copy.11
  8.8 1.0 fusion.6
  9.8 1.0 fusion.8
  10.8 0.1 concatenate.20
  10.9 5.1 %collective-permute-start = (bf16[16,2562]{1,0:T(8,128)(2,1)S(1)}, bf16[16,2562]{1,0:T(8,128)(2,1)S(1)}, u32[]{:S(2)}, u32[]{:S(2)}) collective-permute-start(bf16[16,2562]{1,0:T(8,128)(2,1)S(1)} %concatenate.20), channel_id=1, source_target_pairs={{0,1},{1,0},{2,3},{3,2},{4,5},{5,4},{6,7},{7,6},{8,9},{9,8},{10,11... | collective-permute-start | bytes 245960 | tf_op jit(solution)/shard_map/ppermute | solution.py:14
  16.1 2.7 %collective-permute-done = bf16[16,2562]{1,0:T(8,128)(2,1)S(1)} collective-permute-done((bf16[16,2562]{1,0:T(8,128)(2,1)S(1)}, bf16[16,2562]{1,0:T(8,128)(2,1)S(1)}, u32[]{:S(2)}, u32[]{:S(2)}) %collective-permute-start) | collective-permute-done | bytes 82016 | tf_op jit(solution)/shard_map/ppermute | solution.py:14
  18.8 3.8 %collective-permute-start.1 = (bf16[32,2562]{1,0:T(8,128)(2,1)S(1)}, bf16[32,2562]{1,0:T(8,128)(2,1)S(1)}, u32[]{:S(2)}, u32[]{:S(2)}) collective-permute-start(bf16[32,2562]{1,0:T(8,128)(2,1)S(1)} %pad_maximum_fusion), channel_id=1, source_target_pairs={{0,2},{2,4},{4,6},{6,8},{8,10},{10,12},{12,14},{14,16},{16,18},{18... | collective-permute-start | bytes 491912 | tf_op jit(solution)/shard_map/ppermute | solution.py:14
  22.6 9.5 %collective-permute-start.7 = (bf16[32,2562]{1,0:T(8,128)(2,1)S(1)}, bf16[32,2562]{1,0:T(8,128)(2,1)S(1)}, u32[]{:S(2)}, u32[]{:S(2)}) collective-permute-start(bf16[32,2562]{1,0:T(8,128)(2,1)S(1)} %pad_maximum_fusion), channel_id=1, source_target_pairs={{0,30},{2,0},{4,2},{6,4},{8,6},{10,8},{12,10},{14,12},{16,14},{18,... | collective-permute-start | bytes 491912 | tf_op jit(solution)/shard_map/ppermute | solution.py:14
  32.1 1.4 collective-permute-done.1
  33.5 1.9 %collective-permute-start.2 = (bf16[32,2562]{1,0:T(8,128)(2,1)S(1)}, bf16[32,2562]{1,0:T(8,128)(2,1)S(1)}, u32[]{:S(2)}, u32[]{:S(2)}) collective-permute-start(bf16[32,2562]{1,0:T(8,128)(2,1)S(1)} %collective-permute-done.1), channel_id=1, source_target_pairs={{0,2},{2,4},{4,6},{6,8},{8,10},{10,12},{12,14},{14,16},{16,18},{18... | collective-permute-start | bytes 491912 | tf_op jit(solution)/shard_map/ppermute | solution.py:14
  35.5 5.1 %collective-permute-start.8 = (bf16[32,2562]{1,0:T(8,128)(2,1)S(1)}, bf16[32,2562]{1,0:T(8,128)(2,1)S(1)}, u32[]{:S(2)}, u32[]{:S(2)}) collective-permute-start(bf16[32,2562]{1,0:T(8,128)(2,1)S(1)} %collective-permute-done.7), channel_id=1, source_target_pairs={{0,30},{2,0},{4,2},{6,4},{8,6},{10,8},{12,10},{14,12},{16,14},{18,... | collective-permute-start | bytes 491912 | tf_op jit(solution)/shard_map/ppermute | solution.py:14
  40.6 1.4 collective-permute-done.2
  42.0 1.9 %collective-permute-start.3 = (bf16[32,2562]{1,0:T(8,128)(2,1)S(1)}, bf16[32,2562]{1,0:T(8,128)(2,1)S(1)}, u32[]{:S(2)}, u32[]{:S(2)}) collective-permute-start(bf16[32,2562]{1,0:T(8,128)(2,1)S(1)} %collective-permute-done.2), channel_id=1, source_target_pairs={{0,2},{2,4},{4,6},{6,8},{8,10},{10,12},{12,14},{14,16},{16,18},{18... | collective-permute-start | bytes 491912 | tf_op jit(solution)/shard_map/ppermute | solution.py:14
  44.0 5.1 %collective-permute-start.9 = (bf16[32,2562]{1,0:T(8,128)(2,1)S(1)}, bf16[32,2562]{1,0:T(8,128)(2,1)S(1)}, u32[]{:S(2)}, u32[]{:S(2)}) collective-permute-start(bf16[32,2562]{1,0:T(8,128)(2,1)S(1)} %collective-permute-done.8), channel_id=1, source_target_pairs={{0,30},{2,0},{4,2},{6,4},{8,6},{10,8},{12,10},{14,12},{16,14},{18,... | collective-permute-start | bytes 491912 | tf_op jit(solution)/shard_map/ppermute | solution.py:14
  49.1 41.1 %all-gather.2.cloned.1.call-done = bf16[2560,1024]{1,0:T(8,128)(2,1)} async-done(((bf16[2560,128]{1,0:T(8,128)(2,1)}), bf16[2560,1024]{1,0:T(8,128)(2,1)}) %all-gather.2.cloned.1.call-update) | async-done | bytes 5242896 | tf_op jit(solution)/shard_map/all_gather | solution.py:61
  90.2 1.9 %collective-permute-start.13 = (bf16[2560,1024]{1,0:T(8,128)(2,1)}, bf16[2560,1024]{1,0:T(8,128)(2,1)S(1)}, u32[]{:S(2)}, u32[]{:S(2)}) collective-permute-start(bf16[2560,1024]{1,0:T(8,128)(2,1)} %all-gather.2.cloned.1.call-done), channel_id=1, source_target_pairs={{0,32},{32,0},{1,33},{33,1},{2,34},{34,2},{3,35},{35,3},{4,36},{36... | collective-permute-start | bytes 15728648 | tf_op jit(solution)/shard_map/ppermute | solution.py:14
  92.2 3.5 %collective-permute-start.4 = (bf16[32,2562]{1,0:T(8,128)(2,1)S(1)}, bf16[32,2562]{1,0:T(8,128)(2,1)S(1)}, u32[]{:S(2)}, u32[]{:S(2)}) collective-permute-start(bf16[32,2562]{1,0:T(8,128)(2,1)S(1)} %collective-permute-done.3), channel_id=1, source_target_pairs={{0,2},{2,4},{4,6},{6,8},{8,10},{10,12},{12,14},{14,16},{16,18},{18... | collective-permute-start | bytes 491912 | tf_op jit(solution)/shard_map/ppermute | solution.py:14
  95.7 4.4 %collective-permute-start.10 = (bf16[32,2562]{1,0:T(8,128)(2,1)S(1)}, bf16[32,2562]{1,0:T(8,128)(2,1)S(1)}, u32[]{:S(2)}, u32[]{:S(2)}) collective-permute-start(bf16[32,2562]{1,0:T(8,128)(2,1)S(1)} %collective-permute-done.9), channel_id=1, source_target_pairs={{0,30},{2,0},{4,2},{6,4},{8,6},{10,8},{12,10},{14,12},{16,14},{18,... | collective-permute-start | bytes 491912 | tf_op jit(solution)/shard_map/ppermute | solution.py:14
  100.1 3.1 %collective-permute-done.4 = bf16[32,2562]{1,0:T(8,128)(2,1)S(1)} collective-permute-done((bf16[32,2562]{1,0:T(8,128)(2,1)S(1)}, bf16[32,2562]{1,0:T(8,128)(2,1)S(1)}, u32[]{:S(2)}, u32[]{:S(2)}) %collective-permute-start.4) | collective-permute-done | bytes 164000 | tf_op jit(solution)/shard_map/ppermute | solution.py:14
  103.2 1.9 %collective-permute-start.5 = (bf16[32,2562]{1,0:T(8,128)(2,1)S(1)}, bf16[32,2562]{1,0:T(8,128)(2,1)S(1)}, u32[]{:S(2)}, u32[]{:S(2)}) collective-permute-start(bf16[32,2562]{1,0:T(8,128)(2,1)S(1)} %collective-permute-done.4), channel_id=1, source_target_pairs={{0,2},{2,4},{4,6},{6,8},{8,10},{10,12},{12,14},{14,16},{16,18},{18... | collective-permute-start | bytes 491912 | tf_op jit(solution)/shard_map/ppermute | solution.py:14
  105.1 5.1 %collective-permute-start.11 = (bf16[32,2562]{1,0:T(8,128)(2,1)S(1)}, bf16[32,2562]{1,0:T(8,128)(2,1)S(1)}, u32[]{:S(2)}, u32[]{:S(2)}) collective-permute-start(bf16[32,2562]{1,0:T(8,128)(2,1)S(1)} %collective-permute-done.10), channel_id=1, source_target_pairs={{0,30},{2,0},{4,2},{6,4},{8,6},{10,8},{12,10},{14,12},{16,14},{18,... | collective-permute-start | bytes 491912 | tf_op jit(solution)/shard_map/ppermute | solution.py:14
  110.2 2.2 %collective-permute-done.5 = bf16[32,2562]{1,0:T(8,128)(2,1)S(1)} collective-permute-done((bf16[32,2562]{1,0:T(8,128)(2,1)S(1)}, bf16[32,2562]{1,0:T(8,128)(2,1)S(1)}, u32[]{:S(2)}, u32[]{:S(2)}) %collective-permute-start.5) | collective-permute-done | bytes 164000 | tf_op jit(solution)/shard_map/ppermute | solution.py:14
  112.4 1.9 %collective-permute-start.6 = (bf16[32,2562]{1,0:T(8,128)(2,1)S(1)}, bf16[32,2562]{1,0:T(8,128)(2,1)S(1)}, u32[]{:S(2)}, u32[]{:S(2)}) collective-permute-start(bf16[32,2562]{1,0:T(8,128)(2,1)S(1)} %collective-permute-done.5), channel_id=1, source_target_pairs={{0,2},{2,4},{4,6},{6,8},{8,10},{10,12},{12,14},{14,16},{16,18},{18... | collective-permute-start | bytes 491912 | tf_op jit(solution)/shard_map/ppermute | solution.py:14
  114.4 5.1 %collective-permute-start.12 = (bf16[32,2562]{1,0:T(8,128)(2,1)S(1)}, bf16[32,2562]{1,0:T(8,128)(2,1)S(1)}, u32[]{:S(2)}, u32[]{:S(2)}) collective-permute-start(bf16[32,2562]{1,0:T(8,128)(2,1)S(1)} %collective-permute-done.11), channel_id=1, source_target_pairs={{0,30},{2,0},{4,2},{6,4},{8,6},{10,8},{12,10},{14,12},{16,14},{18,... | collective-permute-start | bytes 491912 | tf_op jit(solution)/shard_map/ppermute | solution.py:14
  119.5 1.4 collective-permute-done.6
  120.9 1.9 %collective-permute-start.14 = (bf16[32,2562]{1,0:T(8,128)(2,1)S(1)}, bf16[32,2562]{1,0:T(8,128)(2,1)S(1)}, u32[]{:S(2)}, u32[]{:S(2)}) collective-permute-start(bf16[32,2562]{1,0:T(8,128)(2,1)S(1)} %collective-permute-done.6), channel_id=1, source_target_pairs={{0,2},{2,4},{4,6},{6,8},{8,10},{10,12},{12,14},{14,16},{16,18},{18... | collective-permute-start | bytes 491912 | tf_op jit(solution)/shard_map/ppermute | solution.py:14
  122.9 5.1 %collective-permute-start.16 = (bf16[32,2562]{1,0:T(8,128)(2,1)S(1)}, bf16[32,2562]{1,0:T(8,128)(2,1)S(1)}, u32[]{:S(2)}, u32[]{:S(2)}) collective-permute-start(bf16[32,2562]{1,0:T(8,128)(2,1)S(1)} %collective-permute-done.12), channel_id=1, source_target_pairs={{0,30},{2,0},{4,2},{6,4},{8,6},{10,8},{12,10},{14,12},{16,14},{18,... | collective-permute-start | bytes 491912 | tf_op jit(solution)/shard_map/ppermute | solution.py:14
  128.2 0.2 add_reduce_fusion
  128.4 1.0 collective-permute-done.14
  129.4 1.9 %collective-permute-start.15 = (bf16[32,2562]{1,0:T(8,128)(2,1)S(1)}, bf16[32,2562]{1,0:T(8,128)(2,1)S(1)}, u32[]{:S(2)}, u32[]{:S(2)}) collective-permute-start(bf16[32,2562]{1,0:T(8,128)(2,1)S(1)} %collective-permute-done.14), channel_id=1, source_target_pairs={{0,2},{2,4},{4,6},{6,8},{8,10},{10,12},{12,14},{14,16},{16,18},{18... | collective-permute-start | bytes 491912 | tf_op jit(solution)/shard_map/ppermute | solution.py:14
  131.4 6.6 %collective-permute-done.15 = bf16[32,2562]{1,0:T(8,128)(2,1)S(1)} collective-permute-done((bf16[32,2562]{1,0:T(8,128)(2,1)S(1)}, bf16[32,2562]{1,0:T(8,128)(2,1)S(1)}, u32[]{:S(2)}, u32[]{:S(2)}) %collective-permute-start.15) | collective-permute-done | bytes 164000 | tf_op jit(solution)/shard_map/ppermute | solution.py:14
  138.0 0.2 add_reduce_fusion.1
  138.2 3.3 %constant_dynamic-update-slice_fusion.15 = bf16[2560,2048]{1,0:T(8,128)(2,1)S(1)} fusion(bf16[2560,1024]{1,0:T(8,128)(2,1)} %all-gather.2.cloned.1.call-done), kind=kLoop, calls=%fused_computation.37 | loop fusion | bytes 10485760
  141.5 0.8 constant_dynamic-update-slice_fusion.14
  142.4 4.7 %fusion.43 = (f32[416]{0:T(512)S(1)}, f32[416,2048]{1,0:T(8,128)S(1)}) fusion(bf16[2560,2048]{1,0:T(8,128)(2,1)S(1)} %constant_dynamic-update-slice_fusion.14, bf16[416,2562]{1,0:T(8,128)(2,1)S(1)} %constant_dynamic-update-slice_fusion), kind=kOutput, calls=%fused_computation.133 | convolution fusion | flops 4362927616 | bytes 16025216 | tf_op jit(solution)/shard_map/dot_general | solution.py:22
  147.0 1.9 %fusion.44 = (f32[96]{0:T(128)S(1)}, f32[96,2048]{1,0:T(8,128)S(1)}) fusion(bf16[2560,2048]{1,0:T(8,128)(2,1)S(1)} %constant_dynamic-update-slice_fusion.14, bf16[96,2562]{1,0:T(8,128)(2,1)S(1)} %constant_dynamic-update-slice_fusion.16), kind=kOutput, calls=%fused_computation.134 | convolution fusion | flops 1006829440 | bytes 11764096 | tf_op jit(solution)/shard_map/dot_general | solution.py:22
  148.9 1.4 fusion
  150.5 0.4 fusion.3
  150.9 0.1 pad_maximum_fusion.2
  150.9 0.1 reshape.286
  151.1 0.6 gather_fusion
  151.7 0.1 select_bitcast_fusion
  151.8 28.4 %all_to_all.5 = f32[3,32,16]{2,0,1:T(4,128)S(1)} all-to-all(f32[3,32,16]{2,0,1:T(4,128)S(1)} %select_bitcast_fusion), channel_id=1, replica_groups=mesh['ylo'=2,'x'=4,'core'=2,'z'=16,'yhi'=2] {'z','yhi'}, dimensions={1} | all-to-all | bytes 12288 | tf_op jit(solution)/shard_map/all_to_all | solution.py:89
  180.3 0.5 convert_multiply_fusion.2
  180.9 0.5 subtract_multiply_fusion
  (45 shorter events, 0.8 us)
Async XLA Ops:
  7.2 83.1 %all-gather.2.cloned.1.call-start = ((), (), s32[]{:S(2)}) async-start(), calls=%async_computation.1 | async-start | bytes 5898240 | tf_op jit(solution)/shard_map/all_gather | solution.py:61
  10.9 7.9 %collective-permute-start = (bf16[16,2562]{1,0:T(8,128)(2,1)S(1)}, bf16[16,2562]{1,0:T(8,128)(2,1)S(1)}, u32[]{:S(2)}, u32[]{:S(2)}) collective-permute-start(bf16[16,2562]{1,0:T(8,128)(2,1)S(1)} %concatenate.20), channel_id=1, source_target_pairs={{0,1},{1,0},{2,3},{3,2},{4,5},{5,4},{6,7},{7,6},{8,9},{9,8},{10,11... | collective-permute-start | bytes 245960 | tf_op jit(solution)/shard_map/ppermute | solution.py:14
  18.8 14.8 %collective-permute-start.1 = (bf16[32,2562]{1,0:T(8,128)(2,1)S(1)}, bf16[32,2562]{1,0:T(8,128)(2,1)S(1)}, u32[]{:S(2)}, u32[]{:S(2)}) collective-permute-start(bf16[32,2562]{1,0:T(8,128)(2,1)S(1)} %pad_maximum_fusion), channel_id=1, source_target_pairs={{0,2},{2,4},{4,6},{6,8},{8,10},{10,12},{12,14},{14,16},{16,18},{18... | collective-permute-start | bytes 491912 | tf_op jit(solution)/shard_map/ppermute | solution.py:14
  22.6 12.9 %collective-permute-start.7 = (bf16[32,2562]{1,0:T(8,128)(2,1)S(1)}, bf16[32,2562]{1,0:T(8,128)(2,1)S(1)}, u32[]{:S(2)}, u32[]{:S(2)}) collective-permute-start(bf16[32,2562]{1,0:T(8,128)(2,1)S(1)} %pad_maximum_fusion), channel_id=1, source_target_pairs={{0,30},{2,0},{4,2},{6,4},{8,6},{10,8},{12,10},{14,12},{16,14},{18,... | collective-permute-start | bytes 491912 | tf_op jit(solution)/shard_map/ppermute | solution.py:14
  33.5 8.5 %collective-permute-start.2 = (bf16[32,2562]{1,0:T(8,128)(2,1)S(1)}, bf16[32,2562]{1,0:T(8,128)(2,1)S(1)}, u32[]{:S(2)}, u32[]{:S(2)}) collective-permute-start(bf16[32,2562]{1,0:T(8,128)(2,1)S(1)} %collective-permute-done.1), channel_id=1, source_target_pairs={{0,2},{2,4},{4,6},{6,8},{8,10},{10,12},{12,14},{14,16},{16,18},{18... | collective-permute-start | bytes 491912 | tf_op jit(solution)/shard_map/ppermute | solution.py:14
  35.5 8.5 %collective-permute-start.8 = (bf16[32,2562]{1,0:T(8,128)(2,1)S(1)}, bf16[32,2562]{1,0:T(8,128)(2,1)S(1)}, u32[]{:S(2)}, u32[]{:S(2)}) collective-permute-start(bf16[32,2562]{1,0:T(8,128)(2,1)S(1)} %collective-permute-done.7), channel_id=1, source_target_pairs={{0,30},{2,0},{4,2},{6,4},{8,6},{10,8},{12,10},{14,12},{16,14},{18,... | collective-permute-start | bytes 491912 | tf_op jit(solution)/shard_map/ppermute | solution.py:14
  42.0 50.1 %collective-permute-start.3 = (bf16[32,2562]{1,0:T(8,128)(2,1)S(1)}, bf16[32,2562]{1,0:T(8,128)(2,1)S(1)}, u32[]{:S(2)}, u32[]{:S(2)}) collective-permute-start(bf16[32,2562]{1,0:T(8,128)(2,1)S(1)} %collective-permute-done.2), channel_id=1, source_target_pairs={{0,2},{2,4},{4,6},{6,8},{8,10},{10,12},{12,14},{14,16},{16,18},{18... | collective-permute-start | bytes 491912 | tf_op jit(solution)/shard_map/ppermute | solution.py:14
  44.0 51.7 %collective-permute-start.9 = (bf16[32,2562]{1,0:T(8,128)(2,1)S(1)}, bf16[32,2562]{1,0:T(8,128)(2,1)S(1)}, u32[]{:S(2)}, u32[]{:S(2)}) collective-permute-start(bf16[32,2562]{1,0:T(8,128)(2,1)S(1)} %collective-permute-done.8), channel_id=1, source_target_pairs={{0,30},{2,0},{4,2},{6,4},{8,6},{10,8},{12,10},{14,12},{16,14},{18,... | collective-permute-start | bytes 491912 | tf_op jit(solution)/shard_map/ppermute | solution.py:14
  90.2 51.3 %collective-permute-start.13 = (bf16[2560,1024]{1,0:T(8,128)(2,1)}, bf16[2560,1024]{1,0:T(8,128)(2,1)S(1)}, u32[]{:S(2)}, u32[]{:S(2)}) collective-permute-start(bf16[2560,1024]{1,0:T(8,128)(2,1)} %all-gather.2.cloned.1.call-done), channel_id=1, source_target_pairs={{0,32},{32,0},{1,33},{33,1},{2,34},{34,2},{3,35},{35,3},{4,36},{36... | collective-permute-start | bytes 15728648 | tf_op jit(solution)/shard_map/ppermute | solution.py:14
  92.2 11.0 %collective-permute-start.4 = (bf16[32,2562]{1,0:T(8,128)(2,1)S(1)}, bf16[32,2562]{1,0:T(8,128)(2,1)S(1)}, u32[]{:S(2)}, u32[]{:S(2)}) collective-permute-start(bf16[32,2562]{1,0:T(8,128)(2,1)S(1)} %collective-permute-done.3), channel_id=1, source_target_pairs={{0,2},{2,4},{4,6},{6,8},{8,10},{10,12},{12,14},{14,16},{16,18},{18... | collective-permute-start | bytes 491912 | tf_op jit(solution)/shard_map/ppermute | solution.py:14
  95.7 9.4 %collective-permute-start.10 = (bf16[32,2562]{1,0:T(8,128)(2,1)S(1)}, bf16[32,2562]{1,0:T(8,128)(2,1)S(1)}, u32[]{:S(2)}, u32[]{:S(2)}) collective-permute-start(bf16[32,2562]{1,0:T(8,128)(2,1)S(1)} %collective-permute-done.9), channel_id=1, source_target_pairs={{0,30},{2,0},{4,2},{6,4},{8,6},{10,8},{12,10},{14,12},{16,14},{18,... | collective-permute-start | bytes 491912 | tf_op jit(solution)/shard_map/ppermute | solution.py:14
  103.2 9.3 %collective-permute-start.5 = (bf16[32,2562]{1,0:T(8,128)(2,1)S(1)}, bf16[32,2562]{1,0:T(8,128)(2,1)S(1)}, u32[]{:S(2)}, u32[]{:S(2)}) collective-permute-start(bf16[32,2562]{1,0:T(8,128)(2,1)S(1)} %collective-permute-done.4), channel_id=1, source_target_pairs={{0,2},{2,4},{4,6},{6,8},{8,10},{10,12},{12,14},{14,16},{16,18},{18... | collective-permute-start | bytes 491912 | tf_op jit(solution)/shard_map/ppermute | solution.py:14
  105.1 9.3 %collective-permute-start.11 = (bf16[32,2562]{1,0:T(8,128)(2,1)S(1)}, bf16[32,2562]{1,0:T(8,128)(2,1)S(1)}, u32[]{:S(2)}, u32[]{:S(2)}) collective-permute-start(bf16[32,2562]{1,0:T(8,128)(2,1)S(1)} %collective-permute-done.10), channel_id=1, source_target_pairs={{0,30},{2,0},{4,2},{6,4},{8,6},{10,8},{12,10},{14,12},{16,14},{18,... | collective-permute-start | bytes 491912 | tf_op jit(solution)/shard_map/ppermute | solution.py:14
  112.4 8.5 %collective-permute-start.6 = (bf16[32,2562]{1,0:T(8,128)(2,1)S(1)}, bf16[32,2562]{1,0:T(8,128)(2,1)S(1)}, u32[]{:S(2)}, u32[]{:S(2)}) collective-permute-start(bf16[32,2562]{1,0:T(8,128)(2,1)S(1)} %collective-permute-done.5), channel_id=1, source_target_pairs={{0,2},{2,4},{4,6},{6,8},{8,10},{10,12},{12,14},{14,16},{16,18},{18... | collective-permute-start | bytes 491912 | tf_op jit(solution)/shard_map/ppermute | solution.py:14
  114.4 8.5 %collective-permute-start.12 = (bf16[32,2562]{1,0:T(8,128)(2,1)S(1)}, bf16[32,2562]{1,0:T(8,128)(2,1)S(1)}, u32[]{:S(2)}, u32[]{:S(2)}) collective-permute-start(bf16[32,2562]{1,0:T(8,128)(2,1)S(1)} %collective-permute-done.11), channel_id=1, source_target_pairs={{0,30},{2,0},{4,2},{6,4},{8,6},{10,8},{12,10},{14,12},{16,14},{18,... | collective-permute-start | bytes 491912 | tf_op jit(solution)/shard_map/ppermute | solution.py:14
  120.9 8.5 %collective-permute-start.14 = (bf16[32,2562]{1,0:T(8,128)(2,1)S(1)}, bf16[32,2562]{1,0:T(8,128)(2,1)S(1)}, u32[]{:S(2)}, u32[]{:S(2)}) collective-permute-start(bf16[32,2562]{1,0:T(8,128)(2,1)S(1)} %collective-permute-done.6), channel_id=1, source_target_pairs={{0,2},{2,4},{4,6},{6,8},{8,10},{10,12},{12,14},{14,16},{16,18},{18... | collective-permute-start | bytes 491912 | tf_op jit(solution)/shard_map/ppermute | solution.py:14
  122.9 15.1 %collective-permute-start.16 = (bf16[32,2562]{1,0:T(8,128)(2,1)S(1)}, bf16[32,2562]{1,0:T(8,128)(2,1)S(1)}, u32[]{:S(2)}, u32[]{:S(2)}) collective-permute-start(bf16[32,2562]{1,0:T(8,128)(2,1)S(1)} %collective-permute-done.12), channel_id=1, source_target_pairs={{0,30},{2,0},{4,2},{6,4},{8,6},{10,8},{12,10},{14,12},{16,14},{18,... | collective-permute-start | bytes 491912 | tf_op jit(solution)/shard_map/ppermute | solution.py:14
  129.4 8.5 %collective-permute-start.15 = (bf16[32,2562]{1,0:T(8,128)(2,1)S(1)}, bf16[32,2562]{1,0:T(8,128)(2,1)S(1)}, u32[]{:S(2)}, u32[]{:S(2)}) collective-permute-start(bf16[32,2562]{1,0:T(8,128)(2,1)S(1)} %collective-permute-done.14), channel_id=1, source_target_pairs={{0,2},{2,4},{4,6},{6,8},{8,10},{10,12},{12,14},{14,16},{16,18},{18... | collective-permute-start | bytes 491912 | tf_op jit(solution)/shard_map/ppermute | solution.py:14
  148.9 31.4 %copy-start = (s32[16]{0:T(128)S(1)}, s32[16]{0:T(128)}, u32[]{:S(2)}) copy-start(s32[16]{0:T(128)} %param.9) | copy-start | bytes 196
Sparse Core Ops, SparseCore 0:
  10.0 80.1 all-gather.1
where the time goes:
time: 189 us; the launch traced here: 188 us
  starting transfers between devices  65.4 us (35%)
  waiting for transfers between devices  61.6 us (33%)
  blocking collectives  28.4 us (15%)
  between operations  14.4 us (8%)
  matrix products  6.55 us (3%)
  other arithmetic  6.35 us (3%)
  local copies, waits for them, and re-layouts  5.6 us (3%)
    ppermute x17, starting transfers between devices, shift(): lax.ppermute(value, axis, [(i, (i + step) % count) for i in range(count)])  65.3 us
    all_gather x1, waiting for transfers between devices, local(): chip_piece = lax.all_gather(head_weight, ('ylo', 'x'), axis=1, tiled=True)  41.1 us
    all_to_all x1, blocking collectives, local(): lax.all_to_all(stats, mp_axes, split_axis=1, concat_axis=1, tiled=True)  28.4 us
    ppermute x17, waiting for transfers between devices, shift(): lax.ppermute(value, axis, [(i, (i + step) % count) for i in range(count)])  19.8 us
    dot_general x2, matrix products, block_stats(): jnp.dot(group_states, column_piece, preferred_element_type=jnp.float32)  6.55 us
  transfers between devices with their start and end apart: 18, of which 9 were waited for; matrix products, arithmetic and copies ran while one was open for 4% of the time, Pallas kernels for 0%

commit v1 on v0

--- a/solution.py
+++ b/solution.py
@@ -51,22 +51,17 @@
     behind = pair
     blocks = [pair]
     returning = []
-    for _ in range(1, z_count // 2):
+    for _ in range(z_count // 2 - 1):
         ahead = shift(ahead, "z", 1)
         behind = shift(behind, "z", -1)
         blocks.append(ahead)
         returning.append(behind)
     blocks.append(shift(ahead, "z", 1))
     ordered = blocks + returning[::-1]
-    chip_piece = lax.all_gather(head_weight, ("ylo", "x"), axis=1, tiled=True)
-    other_piece = shift(chip_piece, "core", 1)
-    column_piece = jnp.concatenate([chip_piece, other_piece], axis=1)
-    core_index = lax.axis_index("core")
+    column_piece = lax.all_gather(head_weight, dp_axes, axis=1, tiled=True)
     positions = jnp.arange(column_piece.shape[1], dtype=jnp.int32)
-    half = positions // chip_piece.shape[1]
-    within = positions % chip_piece.shape[1]
-    owners = (within // shard_cols) * 2 + (half + core_index) % 2
-    column_ids = (owners * mp_count + mp_index) * shard_cols + within % shard_cols
+    owners = positions // shard_cols
+    column_ids = (owners * mp_count + mp_index) * shard_cols + positions % shard_cols
     late = (z_count // 2 - 1, z_count // 2, z_count // 2 + 1)
     early = [k for k in range(z_count) if k not in late]
     early_stats = block_stats(
@@ -75,16 +70,14 @@
     late_stats = block_stats(
         jnp.concatenate([ordered[k] for k in late], axis=0), column_piece, column_ids, width
     )
-    block_rows = pair.shape[0]
-    pieces = {}
-    for i, k in enumerate(early):
-        pieces[k] = early_stats[:, i * block_rows:(i + 1) * block_rows]
-    for i, k in enumerate(late):
-        pieces[k] = late_stats[:, i * block_rows:(i + 1) * block_rows]
-    stats = jnp.concatenate([pieces[k] for k in range(z_count)], axis=1)
+    stats = jnp.concatenate([early_stats, late_stats], axis=1)
     stats = stats.reshape(3, mp_count, send_count)
+    place = [0] * z_count
+    for i, k in enumerate(early + list(late)):
+        place[k] = i
     owner = jnp.arange(mp_count, dtype=jnp.int32)
-    source = ((z_index - owner // 2) % z_count) * 2 + (owner % 2 + yhi_index) % 2
+    block = (z_index - owner // 2) % z_count
+    source = jnp.asarray(place, jnp.int32)[block] * 2 + (owner % 2 + yhi_index) % 2
     stats = jnp.take(stats, source, axis=1)
     got = lax.all_to_all(stats, mp_axes, split_axis=1, concat_axis=1, tiled=True)
     lse_parts, expected_parts, chosen_parts = got[0], got[1], got[2]
@@ -95,7 +88,8 @@
     chosen_logit = jnp.sum(chosen_parts, axis=0)
 
     scored = response_mask.astype(jnp.float32)
-    return ((chosen_logit - log_total) * scored, (log_total - expected) * scored)
+    both = jnp.stack([chosen_logit - log_total, log_total - expected], axis=0) * scored[None, :]
+    return (both[0], both[1])
 
 
 def split_mesh(mesh):

time: 189 us -> 145 us (0.77)
  the two profiles are of different devices: /device:TPU:6 before, /device:TPU:2 now
where the time goes in v1:
time: 145 us; the launch traced here: 144 us
  starting transfers between devices  75.3 us (52%)
  waiting for transfers between devices  35.5 us (24%)
  between operations  14.4 us (10%)
  matrix products  9.54 us (7%)
  other arithmetic  5.96 us (4%)
  local copies, waits for them, and re-layouts  3.23 us (2%)
    ppermute x16, starting transfers between devices, shift(): lax.ppermute(value, axis, [(i, (i + step) % count) for i in range(count)])  63.5 us
    ppermute x16, waiting for transfers between devices, shift(): lax.ppermute(value, axis, [(i, (i + step) % count) for i in range(count)])  19.6 us
    all_to_all x1, waiting for transfers between devices, local(): lax.all_to_all(stats, mp_axes, split_axis=1, concat_axis=1, tiled=True)  15.2 us
    all_to_all x1, starting transfers between devices, local(): lax.all_to_all(stats, mp_axes, split_axis=1, concat_axis=1, tiled=True)  11.8 us
    dot_general x2, matrix products, block_stats(): jnp.dot(group_states, column_piece, preferred_element_type=jnp.float32)  9.54 us
  transfers between devices with their start and end apart: 18, of which 11 were waited for; matrix products, arithmetic and copies ran while one was open for 4% of the time, Pallas kernels for 0%

profile of v1, /device:TPU:2, one launch (start us, length us, event | category | flops | bytes accessed | tf_op | source)
XLA Modules:
  0.0 144.0 jit_solution(13126726183809472267)
XLA Ops:
  7.2 0.7 all-gather.2.cloned.1.call-update
  7.9 0.7 fusion.26
  8.6 0.1 copy.11
  8.7 0.1 copy.12
  8.8 1.0 fusion.6
  9.8 1.0 fusion.8
  10.8 0.1 concatenate.16
  10.9 5.1 %collective-permute-start = (bf16[16,2562]{1,0:T(8,128)(2,1)S(1)}, bf16[16,2562]{1,0:T(8,128)(2,1)S(1)}, u32[]{:S(2)}, u32[]{:S(2)}) collective-permute-start(bf16[16,2562]{1,0:T(8,128)(2,1)S(1)} %concatenate.16), channel_id=1, source_target_pairs={{0,1},{1,0},{2,3},{3,2},{4,5},{5,4},{6,7},{7,6},{8,9},{9,8},{10,11... | collective-permute-start | bytes 245960 | tf_op jit(solution)/shard_map/ppermute | solution.py:14
  16.0 1.4 gather_fusion
  17.4 1.3 collective-permute-done
  18.8 3.8 %collective-permute-start.1 = (bf16[32,2562]{1,0:T(8,128)(2,1)S(1)}, bf16[32,2562]{1,0:T(8,128)(2,1)S(1)}, u32[]{:S(2)}, u32[]{:S(2)}) collective-permute-start(bf16[32,2562]{1,0:T(8,128)(2,1)S(1)} %pad_maximum_fusion), channel_id=1, source_target_pairs={{0,2},{2,4},{4,6},{6,8},{8,10},{10,12},{12,14},{14,16},{16,18},{18... | collective-permute-start | bytes 491912 | tf_op jit(solution)/shard_map/ppermute | solution.py:14
  22.6 9.5 %collective-permute-start.7 = (bf16[32,2562]{1,0:T(8,128)(2,1)S(1)}, bf16[32,2562]{1,0:T(8,128)(2,1)S(1)}, u32[]{:S(2)}, u32[]{:S(2)}) collective-permute-start(bf16[32,2562]{1,0:T(8,128)(2,1)S(1)} %pad_maximum_fusion), channel_id=1, source_target_pairs={{0,30},{2,0},{4,2},{6,4},{8,6},{10,8},{12,10},{14,12},{16,14},{18,... | collective-permute-start | bytes 491912 | tf_op jit(solution)/shard_map/ppermute | solution.py:14
  32.1 1.4 collective-permute-done.1
  33.5 1.9 %collective-permute-start.2 = (bf16[32,2562]{1,0:T(8,128)(2,1)S(1)}, bf16[32,2562]{1,0:T(8,128)(2,1)S(1)}, u32[]{:S(2)}, u32[]{:S(2)}) collective-permute-start(bf16[32,2562]{1,0:T(8,128)(2,1)S(1)} %collective-permute-done.1), channel_id=1, source_target_pairs={{0,2},{2,4},{4,6},{6,8},{8,10},{10,12},{12,14},{14,16},{16,18},{18... | collective-permute-start | bytes 491912 | tf_op jit(solution)/shard_map/ppermute | solution.py:14
  35.5 5.1 %collective-permute-start.8 = (bf16[32,2562]{1,0:T(8,128)(2,1)S(1)}, bf16[32,2562]{1,0:T(8,128)(2,1)S(1)}, u32[]{:S(2)}, u32[]{:S(2)}) collective-permute-start(bf16[32,2562]{1,0:T(8,128)(2,1)S(1)} %collective-permute-done.7), channel_id=1, source_target_pairs={{0,30},{2,0},{4,2},{6,4},{8,6},{10,8},{12,10},{14,12},{16,14},{18,... | collective-permute-start | bytes 491912 | tf_op jit(solution)/shard_map/ppermute | solution.py:14
  40.6 1.4 collective-permute-done.2
  42.0 1.9 %collective-permute-start.3 = (bf16[32,2562]{1,0:T(8,128)(2,1)S(1)}, bf16[32,2562]{1,0:T(8,128)(2,1)S(1)}, u32[]{:S(2)}, u32[]{:S(2)}) collective-permute-start(bf16[32,2562]{1,0:T(8,128)(2,1)S(1)} %collective-permute-done.2), channel_id=1, source_target_pairs={{0,2},{2,4},{4,6},{6,8},{8,10},{10,12},{12,14},{14,16},{16,18},{18... | collective-permute-start | bytes 491912 | tf_op jit(solution)/shard_map/ppermute | solution.py:14
  44.0 5.1 %collective-permute-start.9 = (bf16[32,2562]{1,0:T(8,128)(2,1)S(1)}, bf16[32,2562]{1,0:T(8,128)(2,1)S(1)}, u32[]{:S(2)}, u32[]{:S(2)}) collective-permute-start(bf16[32,2562]{1,0:T(8,128)(2,1)S(1)} %collective-permute-done.8), channel_id=1, source_target_pairs={{0,30},{2,0},{4,2},{6,4},{8,6},{10,8},{12,10},{14,12},{16,14},{18,... | collective-permute-start | bytes 491912 | tf_op jit(solution)/shard_map/ppermute | solution.py:14
  49.1 1.4 collective-permute-done.3
  50.5 1.9 %collective-permute-start.4 = (bf16[32,2562]{1,0:T(8,128)(2,1)S(1)}, bf16[32,2562]{1,0:T(8,128)(2,1)S(1)}, u32[]{:S(2)}, u32[]{:S(2)}) collective-permute-start(bf16[32,2562]{1,0:T(8,128)(2,1)S(1)} %collective-permute-done.3), channel_id=1, source_target_pairs={{0,2},{2,4},{4,6},{6,8},{8,10},{10,12},{12,14},{14,16},{16,18},{18... | collective-permute-start | bytes 491912 | tf_op jit(solution)/shard_map/ppermute | solution.py:14
  52.5 5.1 %collective-permute-start.10 = (bf16[32,2562]{1,0:T(8,128)(2,1)S(1)}, bf16[32,2562]{1,0:T(8,128)(2,1)S(1)}, u32[]{:S(2)}, u32[]{:S(2)}) collective-permute-start(bf16[32,2562]{1,0:T(8,128)(2,1)S(1)} %collective-permute-done.9), channel_id=1, source_target_pairs={{0,30},{2,0},{4,2},{6,4},{8,6},{10,8},{12,10},{14,12},{16,14},{18,... | collective-permute-start | bytes 491912 | tf_op jit(solution)/shard_map/ppermute | solution.py:14
  57.6 1.4 collective-permute-done.4
  59.0 1.9 %collective-permute-start.5 = (bf16[32,2562]{1,0:T(8,128)(2,1)S(1)}, bf16[32,2562]{1,0:T(8,128)(2,1)S(1)}, u32[]{:S(2)}, u32[]{:S(2)}) collective-permute-start(bf16[32,2562]{1,0:T(8,128)(2,1)S(1)} %collective-permute-done.4), channel_id=1, source_target_pairs={{0,2},{2,4},{4,6},{6,8},{8,10},{10,12},{12,14},{14,16},{16,18},{18... | collective-permute-start | bytes 491912 | tf_op jit(solution)/shard_map/ppermute | solution.py:14
  61.0 5.4 %collective-permute-start.11 = (bf16[32,2562]{1,0:T(8,128)(2,1)S(1)}, bf16[32,2562]{1,0:T(8,128)(2,1)S(1)}, u32[]{:S(2)}, u32[]{:S(2)}) collective-permute-start(bf16[32,2562]{1,0:T(8,128)(2,1)S(1)} %collective-permute-done.10), channel_id=1, source_target_pairs={{0,30},{2,0},{4,2},{6,4},{8,6},{10,8},{12,10},{14,12},{16,14},{18,... | collective-permute-start | bytes 491912 | tf_op jit(solution)/shard_map/ppermute | solution.py:14
  66.4 2.3 %collective-permute-done.5 = bf16[32,2562]{1,0:T(8,128)(2,1)S(1)} collective-permute-done((bf16[32,2562]{1,0:T(8,128)(2,1)S(1)}, bf16[32,2562]{1,0:T(8,128)(2,1)S(1)}, u32[]{:S(2)}, u32[]{:S(2)}) %collective-permute-start.5) | collective-permute-done | bytes 164000 | tf_op jit(solution)/shard_map/ppermute | solution.py:14
  68.6 1.9 %collective-permute-start.6 = (bf16[32,2562]{1,0:T(8,128)(2,1)S(1)}, bf16[32,2562]{1,0:T(8,128)(2,1)S(1)}, u32[]{:S(2)}, u32[]{:S(2)}) collective-permute-start(bf16[32,2562]{1,0:T(8,128)(2,1)S(1)} %collective-permute-done.5), channel_id=1, source_target_pairs={{0,2},{2,4},{4,6},{6,8},{8,10},{10,12},{12,14},{14,16},{16,18},{18... | collective-permute-start | bytes 491912 | tf_op jit(solution)/shard_map/ppermute | solution.py:14
  70.5 0.1 collective-permute-done.11
  70.6 5.6 %collective-permute-start.12 = (bf16[32,2562]{1,0:T(8,128)(2,1)S(1)}, bf16[32,2562]{1,0:T(8,128)(2,1)S(1)}, u32[]{:S(2)}, u32[]{:S(2)}) collective-permute-start(bf16[32,2562]{1,0:T(8,128)(2,1)S(1)} %collective-permute-done.11), channel_id=1, source_target_pairs={{0,30},{2,0},{4,2},{6,4},{8,6},{10,8},{12,10},{14,12},{16,14},{18,... | collective-permute-start | bytes 491912 | tf_op jit(solution)/shard_map/ppermute | solution.py:14
  76.2 2.3 %collective-permute-done.6 = bf16[32,2562]{1,0:T(8,128)(2,1)S(1)} collective-permute-done((bf16[32,2562]{1,0:T(8,128)(2,1)S(1)}, bf16[32,2562]{1,0:T(8,128)(2,1)S(1)}, u32[]{:S(2)}, u32[]{:S(2)}) %collective-permute-start.6) | collective-permute-done | bytes 164000 | tf_op jit(solution)/shard_map/ppermute | solution.py:14
  78.6 1.9 %collective-permute-start.13 = (bf16[32,2562]{1,0:T(8,128)(2,1)S(1)}, bf16[32,2562]{1,0:T(8,128)(2,1)S(1)}, u32[]{:S(2)}, u32[]{:S(2)}) collective-permute-start(bf16[32,2562]{1,0:T(8,128)(2,1)S(1)} %collective-permute-done.6), channel_id=1, source_target_pairs={{0,2},{2,4},{4,6},{6,8},{8,10},{10,12},{12,14},{14,16},{16,18},{18... | collective-permute-start | bytes 491912 | tf_op jit(solution)/shard_map/ppermute | solution.py:14
  80.5 5.4 %collective-permute-start.15 = (bf16[32,2562]{1,0:T(8,128)(2,1)S(1)}, bf16[32,2562]{1,0:T(8,128)(2,1)S(1)}, u32[]{:S(2)}, u32[]{:S(2)}) collective-permute-start(bf16[32,2562]{1,0:T(8,128)(2,1)S(1)} %collective-permute-done.12), channel_id=1, source_target_pairs={{0,30},{2,0},{4,2},{6,4},{8,6},{10,8},{12,10},{14,12},{16,14},{18,... | collective-permute-start | bytes 491912 | tf_op jit(solution)/shard_map/ppermute | solution.py:14
  86.0 0.2 add_reduce_fusion
  86.3 1.4 collective-permute-done.13
  87.7 1.9 %collective-permute-start.14 = (bf16[32,2562]{1,0:T(8,128)(2,1)S(1)}, bf16[32,2562]{1,0:T(8,128)(2,1)S(1)}, u32[]{:S(2)}, u32[]{:S(2)}) collective-permute-start(bf16[32,2562]{1,0:T(8,128)(2,1)S(1)} %collective-permute-done.13), channel_id=1, source_target_pairs={{0,2},{2,4},{4,6},{6,8},{8,10},{10,12},{12,14},{14,16},{16,18},{18... | collective-permute-start | bytes 491912 | tf_op jit(solution)/shard_map/ppermute | solution.py:14
  89.6 6.6 %collective-permute-done.14 = bf16[32,2562]{1,0:T(8,128)(2,1)S(1)} collective-permute-done((bf16[32,2562]{1,0:T(8,128)(2,1)S(1)}, bf16[32,2562]{1,0:T(8,128)(2,1)S(1)}, u32[]{:S(2)}, u32[]{:S(2)}) %collective-permute-start.14) | collective-permute-done | bytes 164000 | tf_op jit(solution)/shard_map/ppermute | solution.py:14
  96.2 0.2 add_reduce_fusion.1
  96.4 7.6 %fusion.34 = (f32[416]{0:T(512)S(1)}, f32[416,2048]{1,0:T(8,128)S(1)}) fusion(bf16[2560,2048]{1,0:T(8,128)(2,1)} %all-gather.2.cloned.1.call-done, bf16[416,2562]{1,0:T(8,128)(2,1)S(1)} %constant_dynamic-update-slice_fusion), kind=kOutput, calls=%fused_computation.110 | convolution fusion | flops 4362927616 | bytes 16025216 | tf_op jit(solution)/shard_map/dot_general | solution.py:22
  104.0 1.4 fusion
  105.5 1.9 %fusion.33 = (f32[96]{0:T(128)S(1)}, f32[96,2048]{1,0:T(8,128)S(1)}) fusion(bf16[2560,2048]{1,0:T(8,128)(2,1)S(1)} %copy-done, bf16[96,2562]{1,0:T(8,128)(2,1)S(1)} %constant_dynamic-update-slice_fusion.14), kind=kOutput, calls=%fused_computation.109 | convolution fusion | flops 1006829440 | bytes 11764096 | tf_op jit(solution)/shard_map/dot_general | solution.py:22
  107.4 0.4 fusion.3
  107.9 0.1 maximum_maximum_fusion
  107.9 0.1 reshape.302
  108.1 0.6 gather_fusion.1
  108.7 0.7 select_bitcast_fusion
  109.4 11.8 %all-to-all-start = ((f32[3,32,16]{2,0,1:T(4,128)}), f32[3,32,16]{2,0,1:T(4,128)S(1)}, u32[]{:S(2)}, u32[]{:S(2)}) async-start(f32[3,32,16]{2,0,1:T(4,128)} %select_bitcast_fusion), calls=%async_computation | async-start | bytes 131072 | tf_op jit(solution)/shard_map/all_to_all | solution.py:82
  121.2 15.2 %all-to-all-done = f32[3,32,16]{2,0,1:T(4,128)S(1)} async-done(((f32[3,32,16]{2,0,1:T(4,128)}), f32[3,32,16]{2,0,1:T(4,128)S(1)}, u32[]{:S(2)}, u32[]{:S(2)}) %all-to-all-start) | async-done | bytes 6176 | tf_op jit(solution)/shard_map/all_to_all | solution.py:82
  136.5 0.1 fusion.32
  136.7 0.5 slice_bitcast_fusion
  (47 shorter events, 0.7 us)
Async XLA Ops:
  7.2 89.3 %all-gather.2.cloned.1.call-start = ((), (), s32[]{:S(2)}) async-start(), calls=%async_computation.1 | async-start | bytes 11141120 | tf_op jit(solution)/shard_map/all_gather | solution.py:61
  10.9 7.9 %collective-permute-start = (bf16[16,2562]{1,0:T(8,128)(2,1)S(1)}, bf16[16,2562]{1,0:T(8,128)(2,1)S(1)}, u32[]{:S(2)}, u32[]{:S(2)}) collective-permute-start(bf16[16,2562]{1,0:T(8,128)(2,1)S(1)} %concatenate.16), channel_id=1, source_target_pairs={{0,1},{1,0},{2,3},{3,2},{4,5},{5,4},{6,7},{7,6},{8,9},{9,8},{10,11... | collective-permute-start | bytes 245960 | tf_op jit(solution)/shard_map/ppermute | solution.py:14
  18.8 14.8 %collective-permute-start.1 = (bf16[32,2562]{1,0:T(8,128)(2,1)S(1)}, bf16[32,2562]{1,0:T(8,128)(2,1)S(1)}, u32[]{:S(2)}, u32[]{:S(2)}) collective-permute-start(bf16[32,2562]{1,0:T(8,128)(2,1)S(1)} %pad_maximum_fusion), channel_id=1, source_target_pairs={{0,2},{2,4},{4,6},{6,8},{8,10},{10,12},{12,14},{14,16},{16,18},{18... | collective-permute-start | bytes 491912 | tf_op jit(solution)/shard_map/ppermute | solution.py:14
  22.6 12.9 %collective-permute-start.7 = (bf16[32,2562]{1,0:T(8,128)(2,1)S(1)}, bf16[32,2562]{1,0:T(8,128)(2,1)S(1)}, u32[]{:S(2)}, u32[]{:S(2)}) collective-permute-start(bf16[32,2562]{1,0:T(8,128)(2,1)S(1)} %pad_maximum_fusion), channel_id=1, source_target_pairs={{0,30},{2,0},{4,2},{6,4},{8,6},{10,8},{12,10},{14,12},{16,14},{18,... | collective-permute-start | bytes 491912 | tf_op jit(solution)/shard_map/ppermute | solution.py:14
  33.5 8.5 %collective-permute-start.2 = (bf16[32,2562]{1,0:T(8,128)(2,1)S(1)}, bf16[32,2562]{1,0:T(8,128)(2,1)S(1)}, u32[]{:S(2)}, u32[]{:S(2)}) collective-permute-start(bf16[32,2562]{1,0:T(8,128)(2,1)S(1)} %collective-permute-done.1), channel_id=1, source_target_pairs={{0,2},{2,4},{4,6},{6,8},{8,10},{10,12},{12,14},{14,16},{16,18},{18... | collective-permute-start | bytes 491912 | tf_op jit(solution)/shard_map/ppermute | solution.py:14
  35.5 8.5 %collective-permute-start.8 = (bf16[32,2562]{1,0:T(8,128)(2,1)S(1)}, bf16[32,2562]{1,0:T(8,128)(2,1)S(1)}, u32[]{:S(2)}, u32[]{:S(2)}) collective-permute-start(bf16[32,2562]{1,0:T(8,128)(2,1)S(1)} %collective-permute-done.7), channel_id=1, source_target_pairs={{0,30},{2,0},{4,2},{6,4},{8,6},{10,8},{12,10},{14,12},{16,14},{18,... | collective-permute-start | bytes 491912 | tf_op jit(solution)/shard_map/ppermute | solution.py:14
  42.0 8.5 %collective-permute-start.3 = (bf16[32,2562]{1,0:T(8,128)(2,1)S(1)}, bf16[32,2562]{1,0:T(8,128)(2,1)S(1)}, u32[]{:S(2)}, u32[]{:S(2)}) collective-permute-start(bf16[32,2562]{1,0:T(8,128)(2,1)S(1)} %collective-permute-done.2), channel_id=1, source_target_pairs={{0,2},{2,4},{4,6},{6,8},{8,10},{10,12},{12,14},{14,16},{16,18},{18... | collective-permute-start | bytes 491912 | tf_op jit(solution)/shard_map/ppermute | solution.py:14
  44.0 8.5 %collective-permute-start.9 = (bf16[32,2562]{1,0:T(8,128)(2,1)S(1)}, bf16[32,2562]{1,0:T(8,128)(2,1)S(1)}, u32[]{:S(2)}, u32[]{:S(2)}) collective-permute-start(bf16[32,2562]{1,0:T(8,128)(2,1)S(1)} %collective-permute-done.8), channel_id=1, source_target_pairs={{0,30},{2,0},{4,2},{6,4},{8,6},{10,8},{12,10},{14,12},{16,14},{18,... | collective-permute-start | bytes 491912 | tf_op jit(solution)/shard_map/ppermute | solution.py:14
  50.5 8.5 %collective-permute-start.4 = (bf16[32,2562]{1,0:T(8,128)(2,1)S(1)}, bf16[32,2562]{1,0:T(8,128)(2,1)S(1)}, u32[]{:S(2)}, u32[]{:S(2)}) collective-permute-start(bf16[32,2562]{1,0:T(8,128)(2,1)S(1)} %collective-permute-done.3), channel_id=1, source_target_pairs={{0,2},{2,4},{4,6},{6,8},{8,10},{10,12},{12,14},{14,16},{16,18},{18... | collective-permute-start | bytes 491912 | tf_op jit(solution)/shard_map/ppermute | solution.py:14
  52.5 8.5 %collective-permute-start.10 = (bf16[32,2562]{1,0:T(8,128)(2,1)S(1)}, bf16[32,2562]{1,0:T(8,128)(2,1)S(1)}, u32[]{:S(2)}, u32[]{:S(2)}) collective-permute-start(bf16[32,2562]{1,0:T(8,128)(2,1)S(1)} %collective-permute-done.9), channel_id=1, source_target_pairs={{0,30},{2,0},{4,2},{6,4},{8,6},{10,8},{12,10},{14,12},{16,14},{18,... | collective-permute-start | bytes 491912 | tf_op jit(solution)/shard_map/ppermute | solution.py:14
  59.0 9.6 %collective-permute-start.5 = (bf16[32,2562]{1,0:T(8,128)(2,1)S(1)}, bf16[32,2562]{1,0:T(8,128)(2,1)S(1)}, u32[]{:S(2)}, u32[]{:S(2)}) collective-permute-start(bf16[32,2562]{1,0:T(8,128)(2,1)S(1)} %collective-permute-done.4), channel_id=1, source_target_pairs={{0,2},{2,4},{4,6},{6,8},{8,10},{10,12},{12,14},{14,16},{16,18},{18... | collective-permute-start | bytes 491912 | tf_op jit(solution)/shard_map/ppermute | solution.py:14
  61.0 9.6 %collective-permute-start.11 = (bf16[32,2562]{1,0:T(8,128)(2,1)S(1)}, bf16[32,2562]{1,0:T(8,128)(2,1)S(1)}, u32[]{:S(2)}, u32[]{:S(2)}) collective-permute-start(bf16[32,2562]{1,0:T(8,128)(2,1)S(1)} %collective-permute-done.10), channel_id=1, source_target_pairs={{0,30},{2,0},{4,2},{6,4},{8,6},{10,8},{12,10},{14,12},{16,14},{18,... | collective-permute-start | bytes 491912 | tf_op jit(solution)/shard_map/ppermute | solution.py:14
  68.6 9.9 %collective-permute-start.6 = (bf16[32,2562]{1,0:T(8,128)(2,1)S(1)}, bf16[32,2562]{1,0:T(8,128)(2,1)S(1)}, u32[]{:S(2)}, u32[]{:S(2)}) collective-permute-start(bf16[32,2562]{1,0:T(8,128)(2,1)S(1)} %collective-permute-done.5), channel_id=1, source_target_pairs={{0,2},{2,4},{4,6},{6,8},{8,10},{10,12},{12,14},{14,16},{16,18},{18... | collective-permute-start | bytes 491912 | tf_op jit(solution)/shard_map/ppermute | solution.py:14
  70.6 9.9 %collective-permute-start.12 = (bf16[32,2562]{1,0:T(8,128)(2,1)S(1)}, bf16[32,2562]{1,0:T(8,128)(2,1)S(1)}, u32[]{:S(2)}, u32[]{:S(2)}) collective-permute-start(bf16[32,2562]{1,0:T(8,128)(2,1)S(1)} %collective-permute-done.11), channel_id=1, source_target_pairs={{0,30},{2,0},{4,2},{6,4},{8,6},{10,8},{12,10},{14,12},{16,14},{18,... | collective-permute-start | bytes 491912 | tf_op jit(solution)/shard_map/ppermute | solution.py:14
  78.6 9.1 %collective-permute-start.13 = (bf16[32,2562]{1,0:T(8,128)(2,1)S(1)}, bf16[32,2562]{1,0:T(8,128)(2,1)S(1)}, u32[]{:S(2)}, u32[]{:S(2)}) collective-permute-start(bf16[32,2562]{1,0:T(8,128)(2,1)S(1)} %collective-permute-done.6), channel_id=1, source_target_pairs={{0,2},{2,4},{4,6},{6,8},{8,10},{10,12},{12,14},{14,16},{16,18},{18... | collective-permute-start | bytes 491912 | tf_op jit(solution)/shard_map/ppermute | solution.py:14
  80.5 15.7 %collective-permute-start.15 = (bf16[32,2562]{1,0:T(8,128)(2,1)S(1)}, bf16[32,2562]{1,0:T(8,128)(2,1)S(1)}, u32[]{:S(2)}, u32[]{:S(2)}) collective-permute-start(bf16[32,2562]{1,0:T(8,128)(2,1)S(1)} %collective-permute-done.12), channel_id=1, source_target_pairs={{0,30},{2,0},{4,2},{6,4},{8,6},{10,8},{12,10},{14,12},{16,14},{18,... | collective-permute-start | bytes 491912 | tf_op jit(solution)/shard_map/ppermute | solution.py:14
  87.7 8.5 %collective-permute-start.14 = (bf16[32,2562]{1,0:T(8,128)(2,1)S(1)}, bf16[32,2562]{1,0:T(8,128)(2,1)S(1)}, u32[]{:S(2)}, u32[]{:S(2)}) collective-permute-start(bf16[32,2562]{1,0:T(8,128)(2,1)S(1)} %collective-permute-done.13), channel_id=1, source_target_pairs={{0,2},{2,4},{4,6},{6,8},{8,10},{10,12},{12,14},{14,16},{16,18},{18... | collective-permute-start | bytes 491912 | tf_op jit(solution)/shard_map/ppermute | solution.py:14
  96.4 9.0 %copy-start = (bf16[2560,2048]{1,0:T(8,128)(2,1)S(1)}, bf16[2560,2048]{1,0:T(8,128)(2,1)}, u32[]{:S(2)}) copy-start(bf16[2560,2048]{1,0:T(8,128)(2,1)} %all-gather.2.cloned.1.call-done) | copy-start | bytes 31457284
  105.5 15.7 %copy-start.1 = (s32[16]{0:T(128)S(1)}, s32[16]{0:T(128)}, u32[]{:S(2)}) copy-start(s32[16]{0:T(128)} %param.10) | copy-start | bytes 196
  109.4 27.1 %all-to-all-start = ((f32[3,32,16]{2,0,1:T(4,128)}), f32[3,32,16]{2,0,1:T(4,128)S(1)}, u32[]{:S(2)}, u32[]{:S(2)}) async-start(f32[3,32,16]{2,0,1:T(4,128)} %select_bitcast_fusion), calls=%async_computation | async-start | bytes 131072 | tf_op jit(solution)/shard_map/all_to_all | solution.py:82
Sparse Core Ops, SparseCore 0:
  10.0 80.4 all-gather.1

commit v2 on v0

--- a/solution.py
+++ b/solution.py
@@ -51,23 +51,18 @@
     behind = pair
     blocks = [pair]
     returning = []
-    for _ in range(1, z_count // 2):
+    for _ in range(z_count // 2 - 1):
         ahead = shift(ahead, "z", 1)
         behind = shift(behind, "z", -1)
         blocks.append(ahead)
         returning.append(behind)
     blocks.append(shift(ahead, "z", 1))
     ordered = blocks + returning[::-1]
-    chip_piece = lax.all_gather(head_weight, ("ylo", "x"), axis=1, tiled=True)
-    other_piece = shift(chip_piece, "core", 1)
-    column_piece = jnp.concatenate([chip_piece, other_piece], axis=1)
-    core_index = lax.axis_index("core")
+    column_piece = lax.all_gather(head_weight, dp_axes, axis=1, tiled=True)
     positions = jnp.arange(column_piece.shape[1], dtype=jnp.int32)
-    half = positions // chip_piece.shape[1]
-    within = positions % chip_piece.shape[1]
-    owners = (within // shard_cols) * 2 + (half + core_index) % 2
-    column_ids = (owners * mp_count + mp_index) * shard_cols + within % shard_cols
-    late = (z_count // 2 - 1, z_count // 2, z_count // 2 + 1)
+    owners = positions // shard_cols
+    column_ids = (owners * mp_count + mp_index) * shard_cols + positions % shard_cols
+    late = (z_count // 2,)
     early = [k for k in range(z_count) if k not in late]
     early_stats = block_stats(
         jnp.concatenate([ordered[k] for k in early], axis=0), column_piece, column_ids, width

time: 189 us -> 145 us (0.77)
  the two profiles are of different devices: /device:TPU:6 before, /device:TPU:2 now
where the time goes in v2:
time: 145 us; the launch traced here: 144 us
  starting transfers between devices  63.5 us (44%)
  blocking collectives  26.9 us (19%)
  waiting for transfers between devices  21.6 us (15%)
  between operations  14.4 us (10%)
  matrix products  10.3 us (7%)
  other arithmetic  6.41 us (4%)
    ppermute x16, starting transfers between devices, shift(): lax.ppermute(value, axis, [(i, (i + step) % count) for i in range(count)])  63.5 us
    all_to_all x1, blocking collectives, local(): lax.all_to_all(stats, mp_axes, split_axis=1, concat_axis=1, tiled=True)  26.9 us
    ppermute x16, waiting for transfers between devices, shift(): lax.ppermute(value, axis, [(i, (i + step) % count) for i in range(count)])  20.9 us
    dot_general x2, matrix products, block_stats(): jnp.dot(group_states, column_piece, preferred_element_type=jnp.float32)  10.3 us
  transfers between devices with their start and end apart: 17, of which 10 were waited for; matrix products, arithmetic and copies ran while one was open for 3% of the time, Pallas kernels for 0%

profile of v2, /device:TPU:2, one launch (start us, length us, event | category | flops | bytes accessed | tf_op | source)
XLA Modules:
  0.0 144.5 jit_solution(7565106220308004065)
XLA Ops:
  7.2 0.0 all-gather.2.cloned.1.call-start
  7.2 0.7 all-gather.2.cloned.1.call-update
  7.9 0.7 fusion.28
  8.6 0.1 copy.10
  8.7 0.1 copy.11
  8.8 1.0 fusion.4
  9.8 1.0 fusion.6
  10.8 0.1 concatenate.14
  10.9 5.1 %collective-permute-start = (bf16[16,2562]{1,0:T(8,128)(2,1)S(1)}, bf16[16,2562]{1,0:T(8,128)(2,1)S(1)}, u32[]{:S(2)}, u32[]{:S(2)}) collective-permute-start(bf16[16,2562]{1,0:T(8,128)(2,1)S(1)} %concatenate.14), channel_id=1, source_target_pairs={{0,1},{1,0},{2,3},{3,2},{4,5},{5,4},{6,7},{7,6},{8,9},{9,8},{10,11... | collective-permute-start | bytes 245960 | tf_op jit(solution)/shard_map/ppermute | solution.py:14
  16.1 2.7 %collective-permute-done = bf16[16,2562]{1,0:T(8,128)(2,1)S(1)} collective-permute-done((bf16[16,2562]{1,0:T(8,128)(2,1)S(1)}, bf16[16,2562]{1,0:T(8,128)(2,1)S(1)}, u32[]{:S(2)}, u32[]{:S(2)}) %collective-permute-start) | collective-permute-done | bytes 82016 | tf_op jit(solution)/shard_map/ppermute | solution.py:14
  18.8 3.8 %collective-permute-start.1 = (bf16[32,2562]{1,0:T(8,128)(2,1)S(1)}, bf16[32,2562]{1,0:T(8,128)(2,1)S(1)}, u32[]{:S(2)}, u32[]{:S(2)}) collective-permute-start(bf16[32,2562]{1,0:T(8,128)(2,1)S(1)} %pad_maximum_fusion), channel_id=1, source_target_pairs={{0,2},{2,4},{4,6},{6,8},{8,10},{10,12},{12,14},{14,16},{16,18},{18... | collective-permute-start | bytes 491912 | tf_op jit(solution)/shard_map/ppermute | solution.py:14
  22.6 9.5 %collective-permute-start.8 = (bf16[32,2562]{1,0:T(8,128)(2,1)S(1)}, bf16[32,2562]{1,0:T(8,128)(2,1)S(1)}, u32[]{:S(2)}, u32[]{:S(2)}) collective-permute-start(bf16[32,2562]{1,0:T(8,128)(2,1)S(1)} %pad_maximum_fusion), channel_id=1, source_target_pairs={{0,30},{2,0},{4,2},{6,4},{8,6},{10,8},{12,10},{14,12},{16,14},{18,... | collective-permute-start | bytes 491912 | tf_op jit(solution)/shard_map/ppermute | solution.py:14
  32.1 1.4 collective-permute-done.1
  33.5 1.9 %collective-permute-start.2 = (bf16[32,2562]{1,0:T(8,128)(2,1)S(1)}, bf16[32,2562]{1,0:T(8,128)(2,1)S(1)}, u32[]{:S(2)}, u32[]{:S(2)}) collective-permute-start(bf16[32,2562]{1,0:T(8,128)(2,1)S(1)} %collective-permute-done.1), channel_id=1, source_target_pairs={{0,2},{2,4},{4,6},{6,8},{8,10},{10,12},{12,14},{14,16},{16,18},{18... | collective-permute-start | bytes 491912 | tf_op jit(solution)/shard_map/ppermute | solution.py:14
  35.5 5.1 %collective-permute-start.9 = (bf16[32,2562]{1,0:T(8,128)(2,1)S(1)}, bf16[32,2562]{1,0:T(8,128)(2,1)S(1)}, u32[]{:S(2)}, u32[]{:S(2)}) collective-permute-start(bf16[32,2562]{1,0:T(8,128)(2,1)S(1)} %collective-permute-done.8), channel_id=1, source_target_pairs={{0,30},{2,0},{4,2},{6,4},{8,6},{10,8},{12,10},{14,12},{16,14},{18,... | collective-permute-start | bytes 491912 | tf_op jit(solution)/shard_map/ppermute | solution.py:14
  40.6 1.4 collective-permute-done.2
  42.0 1.9 %collective-permute-start.3 = (bf16[32,2562]{1,0:T(8,128)(2,1)S(1)}, bf16[32,2562]{1,0:T(8,128)(2,1)S(1)}, u32[]{:S(2)}, u32[]{:S(2)}) collective-permute-start(bf16[32,2562]{1,0:T(8,128)(2,1)S(1)} %collective-permute-done.2), channel_id=1, source_target_pairs={{0,2},{2,4},{4,6},{6,8},{8,10},{10,12},{12,14},{14,16},{16,18},{18... | collective-permute-start | bytes 491912 | tf_op jit(solution)/shard_map/ppermute | solution.py:14
  44.0 5.1 %collective-permute-start.10 = (bf16[32,2562]{1,0:T(8,128)(2,1)S(1)}, bf16[32,2562]{1,0:T(8,128)(2,1)S(1)}, u32[]{:S(2)}, u32[]{:S(2)}) collective-permute-start(bf16[32,2562]{1,0:T(8,128)(2,1)S(1)} %collective-permute-done.9), channel_id=1, source_target_pairs={{0,30},{2,0},{4,2},{6,4},{8,6},{10,8},{12,10},{14,12},{16,14},{18,... | collective-permute-start | bytes 491912 | tf_op jit(solution)/shard_map/ppermute | solution.py:14
  49.1 1.4 collective-permute-done.3
  50.5 1.9 %collective-permute-start.4 = (bf16[32,2562]{1,0:T(8,128)(2,1)S(1)}, bf16[32,2562]{1,0:T(8,128)(2,1)S(1)}, u32[]{:S(2)}, u32[]{:S(2)}) collective-permute-start(bf16[32,2562]{1,0:T(8,128)(2,1)S(1)} %collective-permute-done.3), channel_id=1, source_target_pairs={{0,2},{2,4},{4,6},{6,8},{8,10},{10,12},{12,14},{14,16},{16,18},{18... | collective-permute-start | bytes 491912 | tf_op jit(solution)/shard_map/ppermute | solution.py:14
  52.5 5.1 %collective-permute-start.11 = (bf16[32,2562]{1,0:T(8,128)(2,1)S(1)}, bf16[32,2562]{1,0:T(8,128)(2,1)S(1)}, u32[]{:S(2)}, u32[]{:S(2)}) collective-permute-start(bf16[32,2562]{1,0:T(8,128)(2,1)S(1)} %collective-permute-done.10), channel_id=1, source_target_pairs={{0,30},{2,0},{4,2},{6,4},{8,6},{10,8},{12,10},{14,12},{16,14},{18,... | collective-permute-start | bytes 491912 | tf_op jit(solution)/shard_map/ppermute | solution.py:14
  57.6 1.4 collective-permute-done.4
  59.0 1.9 %collective-permute-start.5 = (bf16[32,2562]{1,0:T(8,128)(2,1)S(1)}, bf16[32,2562]{1,0:T(8,128)(2,1)S(1)}, u32[]{:S(2)}, u32[]{:S(2)}) collective-permute-start(bf16[32,2562]{1,0:T(8,128)(2,1)S(1)} %collective-permute-done.4), channel_id=1, source_target_pairs={{0,2},{2,4},{4,6},{6,8},{8,10},{10,12},{12,14},{14,16},{16,18},{18... | collective-permute-start | bytes 491912 | tf_op jit(solution)/shard_map/ppermute | solution.py:14
  61.0 5.4 %collective-permute-start.12 = (bf16[32,2562]{1,0:T(8,128)(2,1)S(1)}, bf16[32,2562]{1,0:T(8,128)(2,1)S(1)}, u32[]{:S(2)}, u32[]{:S(2)}) collective-permute-start(bf16[32,2562]{1,0:T(8,128)(2,1)S(1)} %collective-permute-done.11), channel_id=1, source_target_pairs={{0,30},{2,0},{4,2},{6,4},{8,6},{10,8},{12,10},{14,12},{16,14},{18,... | collective-permute-start | bytes 491912 | tf_op jit(solution)/shard_map/ppermute | solution.py:14
  66.4 2.3 %collective-permute-done.5 = bf16[32,2562]{1,0:T(8,128)(2,1)S(1)} collective-permute-done((bf16[32,2562]{1,0:T(8,128)(2,1)S(1)}, bf16[32,2562]{1,0:T(8,128)(2,1)S(1)}, u32[]{:S(2)}, u32[]{:S(2)}) %collective-permute-start.5) | collective-permute-done | bytes 164000 | tf_op jit(solution)/shard_map/ppermute | solution.py:14
  68.6 1.9 %collective-permute-start.6 = (bf16[32,2562]{1,0:T(8,128)(2,1)S(1)}, bf16[32,2562]{1,0:T(8,128)(2,1)S(1)}, u32[]{:S(2)}, u32[]{:S(2)}) collective-permute-start(bf16[32,2562]{1,0:T(8,128)(2,1)S(1)} %collective-permute-done.5), channel_id=1, source_target_pairs={{0,2},{2,4},{4,6},{6,8},{8,10},{10,12},{12,14},{14,16},{16,18},{18... | collective-permute-start | bytes 491912 | tf_op jit(solution)/shard_map/ppermute | solution.py:14
  70.6 0.1 collective-permute-done.12
  70.6 5.6 %collective-permute-start.13 = (bf16[32,2562]{1,0:T(8,128)(2,1)S(1)}, bf16[32,2562]{1,0:T(8,128)(2,1)S(1)}, u32[]{:S(2)}, u32[]{:S(2)}) collective-permute-start(bf16[32,2562]{1,0:T(8,128)(2,1)S(1)} %collective-permute-done.12), channel_id=1, source_target_pairs={{0,30},{2,0},{4,2},{6,4},{8,6},{10,8},{12,10},{14,12},{16,14},{18,... | collective-permute-start | bytes 491912 | tf_op jit(solution)/shard_map/ppermute | solution.py:14
  76.2 2.3 %collective-permute-done.6 = bf16[32,2562]{1,0:T(8,128)(2,1)S(1)} collective-permute-done((bf16[32,2562]{1,0:T(8,128)(2,1)S(1)}, bf16[32,2562]{1,0:T(8,128)(2,1)S(1)}, u32[]{:S(2)}, u32[]{:S(2)}) %collective-permute-start.6) | collective-permute-done | bytes 164000 | tf_op jit(solution)/shard_map/ppermute | solution.py:14
  78.6 1.9 %collective-permute-start.7 = (bf16[32,2562]{1,0:T(8,128)(2,1)S(1)}, bf16[32,2562]{1,0:T(8,128)(2,1)S(1)}, u32[]{:S(2)}, u32[]{:S(2)}) collective-permute-start(bf16[32,2562]{1,0:T(8,128)(2,1)S(1)} %collective-permute-done.6), channel_id=1, source_target_pairs={{0,2},{2,4},{4,6},{6,8},{8,10},{10,12},{12,14},{14,16},{16,18},{18... | collective-permute-start | bytes 491912 | tf_op jit(solution)/shard_map/ppermute | solution.py:14
  80.5 5.4 %collective-permute-start.14 = (bf16[32,2562]{1,0:T(8,128)(2,1)S(1)}, bf16[32,2562]{1,0:T(8,128)(2,1)S(1)}, u32[]{:S(2)}, u32[]{:S(2)}) collective-permute-start(bf16[32,2562]{1,0:T(8,128)(2,1)S(1)} %collective-permute-done.13), channel_id=1, source_target_pairs={{0,30},{2,0},{4,2},{6,4},{8,6},{10,8},{12,10},{14,12},{16,14},{18,... | collective-permute-start | bytes 491912 | tf_op jit(solution)/shard_map/ppermute | solution.py:14
  85.9 1.8 %collective-permute-done.7 = bf16[32,2562]{1,0:T(8,128)(2,1)S(1)} collective-permute-done((bf16[32,2562]{1,0:T(8,128)(2,1)S(1)}, bf16[32,2562]{1,0:T(8,128)(2,1)S(1)}, u32[]{:S(2)}, u32[]{:S(2)}) %collective-permute-start.7) | collective-permute-done | bytes 164000 | tf_op jit(solution)/shard_map/ppermute | solution.py:14
  87.7 1.9 %collective-permute-start.15 = (bf16[32,2562]{1,0:T(8,128)(2,1)S(1)}, bf16[32,2562]{1,0:T(8,128)(2,1)S(1)}, u32[]{:S(2)}, u32[]{:S(2)}) collective-permute-start(bf16[32,2562]{1,0:T(8,128)(2,1)S(1)} %collective-permute-done.7), channel_id=1, source_target_pairs={{0,2},{2,4},{4,6},{6,8},{8,10},{10,12},{12,14},{14,16},{16,18},{18... | collective-permute-start | bytes 491912 | tf_op jit(solution)/shard_map/ppermute | solution.py:14
  89.8 0.2 add_reduce_fusion
  90.0 6.2 %collective-permute-done.15 = bf16[32,2562]{1,0:T(8,128)(2,1)S(1)} collective-permute-done((bf16[32,2562]{1,0:T(8,128)(2,1)S(1)}, bf16[32,2562]{1,0:T(8,128)(2,1)S(1)}, u32[]{:S(2)}, u32[]{:S(2)}) %collective-permute-start.15) | collective-permute-done | bytes 164000 | tf_op jit(solution)/shard_map/ppermute | solution.py:14
  96.2 0.2 add_reduce_fusion.1
  96.4 8.2 %fusion.36 = (f32[480]{0:T(512)S(1)}, f32[480,2048]{1,0:T(8,128)S(1)}) fusion(bf16[2560,2048]{1,0:T(8,128)(2,1)} %all-gather.2.cloned.1.call-done, bf16[480,2562]{1,0:T(8,128)(2,1)S(1)} %constant_dynamic-update-slice_fusion), kind=kOutput, calls=%fused_computation.113 | convolution fusion | flops 5034147328 | bytes 16877440 | tf_op jit(solution)/shard_map/dot_general | solution.py:22
  104.6 1.6 %fusion = (f32[480]{0:T(512)S(1)}, f32[480]{0:T(512)S(1)}, f32[480]{0:T(512)S(1)}) fusion(f32[480,2048]{1,0:T(8,128)S(1)} %get-tuple-element.20, f32[480]{0:T(512)S(1)} %get-tuple-element.19, s32[2048]{0:T(1024)S(1)} %fusion.18, s32[480]{0:T(512)S(1)} %add_reduce_fusion), kind=kLoop, calls=%fused_computation.4 | loop fusion | flops 6879840 | bytes 3949952 | tf_op jit(solution)/shard_map/reduce_sum | solution.py:25
  106.3 2.1 %fusion.37 = (f32[32]{0:T(128)S(1)}, f32[32,2048]{1,0:T(8,128)S(1)}) fusion(bf16[2560,2048]{1,0:T(8,128)(2,1)S(1)} %copy-done, bf16[32,2562]{1,0:T(8,128)(2,1)S(1)} %collective-permute-done.15), kind=kOutput, calls=%fused_computation.114 | convolution fusion | flops 335609824 | bytes 10911872 | tf_op jit(solution)/shard_map/dot_general | solution.py:22
  108.4 0.3 fusion.3
  108.7 0.1 pad_maximum_fusion.2
  108.7 0.1 reshape.246
  108.9 0.6 gather_fusion
  109.5 0.1 select_bitcast_fusion
  109.6 26.9 %all_to_all.5 = f32[3,32,16]{2,0,1:T(4,128)S(1)} all-to-all(f32[3,32,16]{2,0,1:T(4,128)S(1)} %select_bitcast_fusion), channel_id=1, replica_groups=mesh['ylo'=2,'x'=4,'core'=2,'z'=16,'yhi'=2] {'z','yhi'}, dimensions={1} | all-to-all | bytes 12288 | tf_op jit(solution)/shard_map/all_to_all | solution.py:84
  136.5 0.1 fusion.35
  136.6 0.5 convert_multiply_fusion.2
  137.1 0.5 subtract_multiply_fusion
  (42 shorter events, 0.6 us)
Async XLA Ops:
  7.2 89.2 %all-gather.2.cloned.1.call-start = ((), (), s32[]{:S(2)}) async-start(), calls=%async_computation.1 | async-start | bytes 11141120 | tf_op jit(solution)/shard_map/all_gather | solution.py:61
  10.9 7.9 %collective-permute-start = (bf16[16,2562]{1,0:T(8,128)(2,1)S(1)}, bf16[16,2562]{1,0:T(8,128)(2,1)S(1)}, u32[]{:S(2)}, u32[]{:S(2)}) collective-permute-start(bf16[16,2562]{1,0:T(8,128)(2,1)S(1)} %concatenate.14), channel_id=1, source_target_pairs={{0,1},{1,0},{2,3},{3,2},{4,5},{5,4},{6,7},{7,6},{8,9},{9,8},{10,11... | collective-permute-start | bytes 245960 | tf_op jit(solution)/shard_map/ppermute | solution.py:14
  18.8 14.8 %collective-permute-start.1 = (bf16[32,2562]{1,0:T(8,128)(2,1)S(1)}, bf16[32,2562]{1,0:T(8,128)(2,1)S(1)}, u32[]{:S(2)}, u32[]{:S(2)}) collective-permute-start(bf16[32,2562]{1,0:T(8,128)(2,1)S(1)} %pad_maximum_fusion), channel_id=1, source_target_pairs={{0,2},{2,4},{4,6},{6,8},{8,10},{10,12},{12,14},{14,16},{16,18},{18... | collective-permute-start | bytes 491912 | tf_op jit(solution)/shard_map/ppermute | solution.py:14
  22.6 12.9 %collective-permute-start.8 = (bf16[32,2562]{1,0:T(8,128)(2,1)S(1)}, bf16[32,2562]{1,0:T(8,128)(2,1)S(1)}, u32[]{:S(2)}, u32[]{:S(2)}) collective-permute-start(bf16[32,2562]{1,0:T(8,128)(2,1)S(1)} %pad_maximum_fusion), channel_id=1, source_target_pairs={{0,30},{2,0},{4,2},{6,4},{8,6},{10,8},{12,10},{14,12},{16,14},{18,... | collective-permute-start | bytes 491912 | tf_op jit(solution)/shard_map/ppermute | solution.py:14
  33.5 8.5 %collective-permute-start.2 = (bf16[32,2562]{1,0:T(8,128)(2,1)S(1)}, bf16[32,2562]{1,0:T(8,128)(2,1)S(1)}, u32[]{:S(2)}, u32[]{:S(2)}) collective-permute-start(bf16[32,2562]{1,0:T(8,128)(2,1)S(1)} %collective-permute-done.1), channel_id=1, source_target_pairs={{0,2},{2,4},{4,6},{6,8},{8,10},{10,12},{12,14},{14,16},{16,18},{18... | collective-permute-start | bytes 491912 | tf_op jit(solution)/shard_map/ppermute | solution.py:14
  35.5 8.5 %collective-permute-start.9 = (bf16[32,2562]{1,0:T(8,128)(2,1)S(1)}, bf16[32,2562]{1,0:T(8,128)(2,1)S(1)}, u32[]{:S(2)}, u32[]{:S(2)}) collective-permute-start(bf16[32,2562]{1,0:T(8,128)(2,1)S(1)} %collective-permute-done.8), channel_id=1, source_target_pairs={{0,30},{2,0},{4,2},{6,4},{8,6},{10,8},{12,10},{14,12},{16,14},{18,... | collective-permute-start | bytes 491912 | tf_op jit(solution)/shard_map/ppermute | solution.py:14
  42.0 8.5 %collective-permute-start.3 = (bf16[32,2562]{1,0:T(8,128)(2,1)S(1)}, bf16[32,2562]{1,0:T(8,128)(2,1)S(1)}, u32[]{:S(2)}, u32[]{:S(2)}) collective-permute-start(bf16[32,2562]{1,0:T(8,128)(2,1)S(1)} %collective-permute-done.2), channel_id=1, source_target_pairs={{0,2},{2,4},{4,6},{6,8},{8,10},{10,12},{12,14},{14,16},{16,18},{18... | collective-permute-start | bytes 491912 | tf_op jit(solution)/shard_map/ppermute | solution.py:14
  44.0 8.5 %collective-permute-start.10 = (bf16[32,2562]{1,0:T(8,128)(2,1)S(1)}, bf16[32,2562]{1,0:T(8,128)(2,1)S(1)}, u32[]{:S(2)}, u32[]{:S(2)}) collective-permute-start(bf16[32,2562]{1,0:T(8,128)(2,1)S(1)} %collective-permute-done.9), channel_id=1, source_target_pairs={{0,30},{2,0},{4,2},{6,4},{8,6},{10,8},{12,10},{14,12},{16,14},{18,... | collective-permute-start | bytes 491912 | tf_op jit(solution)/shard_map/ppermute | solution.py:14
  50.5 8.5 %collective-permute-start.4 = (bf16[32,2562]{1,0:T(8,128)(2,1)S(1)}, bf16[32,2562]{1,0:T(8,128)(2,1)S(1)}, u32[]{:S(2)}, u32[]{:S(2)}) collective-permute-start(bf16[32,2562]{1,0:T(8,128)(2,1)S(1)} %collective-permute-done.3), channel_id=1, source_target_pairs={{0,2},{2,4},{4,6},{6,8},{8,10},{10,12},{12,14},{14,16},{16,18},{18... | collective-permute-start | bytes 491912 | tf_op jit(solution)/shard_map/ppermute | solution.py:14
  52.5 8.5 %collective-permute-start.11 = (bf16[32,2562]{1,0:T(8,128)(2,1)S(1)}, bf16[32,2562]{1,0:T(8,128)(2,1)S(1)}, u32[]{:S(2)}, u32[]{:S(2)}) collective-permute-start(bf16[32,2562]{1,0:T(8,128)(2,1)S(1)} %collective-permute-done.10), channel_id=1, source_target_pairs={{0,30},{2,0},{4,2},{6,4},{8,6},{10,8},{12,10},{14,12},{16,14},{18,... | collective-permute-start | bytes 491912 | tf_op jit(solution)/shard_map/ppermute | solution.py:14
  59.0 9.6 %collective-permute-start.5 = (bf16[32,2562]{1,0:T(8,128)(2,1)S(1)}, bf16[32,2562]{1,0:T(8,128)(2,1)S(1)}, u32[]{:S(2)}, u32[]{:S(2)}) collective-permute-start(bf16[32,2562]{1,0:T(8,128)(2,1)S(1)} %collective-permute-done.4), channel_id=1, source_target_pairs={{0,2},{2,4},{4,6},{6,8},{8,10},{10,12},{12,14},{14,16},{16,18},{18... | collective-permute-start | bytes 491912 | tf_op jit(solution)/shard_map/ppermute | solution.py:14
  61.0 9.6 %collective-permute-start.12 = (bf16[32,2562]{1,0:T(8,128)(2,1)S(1)}, bf16[32,2562]{1,0:T(8,128)(2,1)S(1)}, u32[]{:S(2)}, u32[]{:S(2)}) collective-permute-start(bf16[32,2562]{1,0:T(8,128)(2,1)S(1)} %collective-permute-done.11), channel_id=1, source_target_pairs={{0,30},{2,0},{4,2},{6,4},{8,6},{10,8},{12,10},{14,12},{16,14},{18,... | collective-permute-start | bytes 491912 | tf_op jit(solution)/shard_map/ppermute | solution.py:14
  68.6 9.9 %collective-permute-start.6 = (bf16[32,2562]{1,0:T(8,128)(2,1)S(1)}, bf16[32,2562]{1,0:T(8,128)(2,1)S(1)}, u32[]{:S(2)}, u32[]{:S(2)}) collective-permute-start(bf16[32,2562]{1,0:T(8,128)(2,1)S(1)} %collective-permute-done.5), channel_id=1, source_target_pairs={{0,2},{2,4},{4,6},{6,8},{8,10},{10,12},{12,14},{14,16},{16,18},{18... | collective-permute-start | bytes 491912 | tf_op jit(solution)/shard_map/ppermute | solution.py:14
  70.6 9.9 %collective-permute-start.13 = (bf16[32,2562]{1,0:T(8,128)(2,1)S(1)}, bf16[32,2562]{1,0:T(8,128)(2,1)S(1)}, u32[]{:S(2)}, u32[]{:S(2)}) collective-permute-start(bf16[32,2562]{1,0:T(8,128)(2,1)S(1)} %collective-permute-done.12), channel_id=1, source_target_pairs={{0,30},{2,0},{4,2},{6,4},{8,6},{10,8},{12,10},{14,12},{16,14},{18,... | collective-permute-start | bytes 491912 | tf_op jit(solution)/shard_map/ppermute | solution.py:14
  78.6 9.1 %collective-permute-start.7 = (bf16[32,2562]{1,0:T(8,128)(2,1)S(1)}, bf16[32,2562]{1,0:T(8,128)(2,1)S(1)}, u32[]{:S(2)}, u32[]{:S(2)}) collective-permute-start(bf16[32,2562]{1,0:T(8,128)(2,1)S(1)} %collective-permute-done.6), channel_id=1, source_target_pairs={{0,2},{2,4},{4,6},{6,8},{8,10},{10,12},{12,14},{14,16},{16,18},{18... | collective-permute-start | bytes 491912 | tf_op jit(solution)/shard_map/ppermute | solution.py:14
  80.5 9.1 %collective-permute-start.14 = (bf16[32,2562]{1,0:T(8,128)(2,1)S(1)}, bf16[32,2562]{1,0:T(8,128)(2,1)S(1)}, u32[]{:S(2)}, u32[]{:S(2)}) collective-permute-start(bf16[32,2562]{1,0:T(8,128)(2,1)S(1)} %collective-permute-done.13), channel_id=1, source_target_pairs={{0,30},{2,0},{4,2},{6,4},{8,6},{10,8},{12,10},{14,12},{16,14},{18,... | collective-permute-start | bytes 491912 | tf_op jit(solution)/shard_map/ppermute | solution.py:14
  87.7 8.5 %collective-permute-start.15 = (bf16[32,2562]{1,0:T(8,128)(2,1)S(1)}, bf16[32,2562]{1,0:T(8,128)(2,1)S(1)}, u32[]{:S(2)}, u32[]{:S(2)}) collective-permute-start(bf16[32,2562]{1,0:T(8,128)(2,1)S(1)} %collective-permute-done.7), channel_id=1, source_target_pairs={{0,2},{2,4},{4,6},{6,8},{8,10},{10,12},{12,14},{14,16},{16,18},{18... | collective-permute-start | bytes 491912 | tf_op jit(solution)/shard_map/ppermute | solution.py:14
  96.4 9.9 %copy-start = (bf16[2560,2048]{1,0:T(8,128)(2,1)S(1)}, bf16[2560,2048]{1,0:T(8,128)(2,1)}, u32[]{:S(2)}) copy-start(bf16[2560,2048]{1,0:T(8,128)(2,1)} %all-gather.2.cloned.1.call-done) | copy-start | bytes 31457284
  106.3 30.3 %copy-start.1 = (s32[16]{0:T(128)S(1)}, s32[16]{0:T(128)}, u32[]{:S(2)}) copy-start(s32[16]{0:T(128)} %param.9) | copy-start | bytes 196
Sparse Core Ops, SparseCore 0:
  10.0 80.4 all-gather.1
